TPU v7x, 512 devices: a whole 4x8x8 slice. The times are simulated.
512 devices in a mesh: req: 64 (over z, x, core), tp: 8 (over y).
Axes of the slice: x: 4, y: 8, z: 8, core: 2. Of those that a mesh axis runs over, the one named last changes fastest.
Arguments:
- q_new: bfloat16 [4096, 5120], P('req', 'tp'), may hold values from -6 to 6
- k_new: bfloat16 [4096, 1024], P('req', 'tp'), may hold values from -15 to 15
- v_new: bfloat16 [4096, 1024], P('req', 'tp'), may hold values from -6 to 6
- k_cache: bfloat16 [1024, 128, 1024], P('req', None, 'tp'), may hold values from -16 to 16
- v_cache: bfloat16 [1024, 128, 1024], P('req', None, 'tp'), may hold values from -6 to 6
- lengths: int32 [32], replicated, may hold values from 1 to 4096, as said below
- page_table: int32 [32, 32], replicated, may hold values from -1 to 1023, as said below
- w_out: bfloat16 [5120, 5120], P('req', 'tp'), may hold values from -0.078125 to 0.078125
Outputs:
- attn_out: bfloat16 [4096, 5120], P('req')
Inputs may be any that keep to these rules, and one draw needn't show every extreme that they name: `lengths`: the last request, 31, has exactly 4096 cached tokens; every request has at least one. `page_table`: request r uses ceil(lengths[r] / 128) logical pages. Its first ceil(ceil(lengths[r] / 128) / 2) logical pages lie among global pages 2r * 16 to (2r + 1) * 16 - 1, the rest among (2r + 1) * 16 to (2r + 2) * 16 - 1; distinct logical pages use distinct global pages; entries past a request's last page are -1.
All inputs are finite; a program needn't handle non-finite values.
Results may differ from a plain program's by a relative error of at most 0.024.
Values may be sent and summed in bfloat16 or wider, within the bound.
No kernel may reach another device: no remote copies, remote signals or barrier semaphores. Data moves between devices by JAX's collectives and lax.ppermute only.
A program may use at most 64 MiB of HBM per device.

v0:
```python
import math
import jax
import jax.numpy as jnp
from jax import lax
from jax.sharding import PartitionSpec as P

HD = 128
GROUP = 5
BLOCK_PAGES = 4
ROPE_BASE = 1000000.0
FLOOR_SCORE = -1e30


def from_partner(value, axis, distance):
    return lax.ppermute(value, axis, [(i, i ^ 1 << distance) for i in range(lax.axis_size(axis))])


def rotate(values, places):
    inverse = 1.0 / ROPE_BASE ** (jnp.arange(0, HD, 2).astype(jnp.float32) / HD)
    angles = places.astype(jnp.float32)[:, None] * inverse[None, :]
    cosine = jnp.concatenate([jnp.cos(angles), jnp.cos(angles)], axis=-1)[:, None, :]
    sine = jnp.concatenate([jnp.sin(angles), jnp.sin(angles)], axis=-1)[:, None, :]
    first_half = values[..., : HD // 2]
    second_half = values[..., HD // 2 :]
    turned = jnp.concatenate([-second_half, first_half], axis=-1)
    return values * cosine + turned * sine


def absorb(state, queries, block_keys, block_values, allowed, scale):
    running_max, running_sum, output = state
    scores = (
        jnp.einsum("qcgd,kcd->cgqk", queries, block_keys, preferred_element_type=jnp.float32)
        * scale
    )
    scores = jnp.where(allowed[None, None], scores, FLOOR_SCORE)
    new_max = jnp.maximum(running_max, jnp.max(scores, axis=-1))
    factor = jnp.exp(running_max - new_max)
    weights = jnp.where(allowed[None, None], jnp.exp(scores - new_max[..., None]), 0.0)
    running_sum = running_sum * factor + jnp.sum(weights, axis=-1)
    mixed = jnp.einsum(
        "cgqk,kcd->qcgd",
        weights.astype(jnp.bfloat16),
        block_values,
        preferred_element_type=jnp.float32,
    )
    output = output * jnp.transpose(factor, (2, 0, 1))[..., None] + mixed
    return (new_max, running_sum, output)


def tensor_total(partial_value):
    return lax.psum(partial_value.astype(jnp.bfloat16), "tp")


def shards(q_new, k_new, v_new, k_cache, v_cache, lengths, page_table, w_out):
    own_rows = q_new.shape[0]
    all_rows = 2 * own_rows
    local_heads = k_new.shape[1] // HD
    pages_local = k_cache.shape[0]
    page_rows = k_cache.shape[1]
    block_rows = BLOCK_PAGES * page_rows
    scale = 1.0 / math.sqrt(HD)
    device_row = lax.axis_index("req")
    parity = device_row % 2
    request = device_row // 2
    length = lengths[request]
    own_places = length + parity * own_rows + jnp.arange(own_rows)
    own_queries = rotate(
        q_new.reshape(own_rows, local_heads * GROUP, HD).astype(jnp.float32), own_places
    ).astype(jnp.bfloat16)
    own_keys = rotate(
        k_new.reshape(own_rows, local_heads, HD).astype(jnp.float32), own_places
    ).astype(jnp.bfloat16)
    own_values = v_new.reshape(own_rows, local_heads, HD)
    peer_queries, peer_keys, peer_values = from_partner(
        (own_queries, own_keys, own_values), "req", 0
    )

    def ordered(mine, theirs):
        return jnp.where(
            parity == 0,
            jnp.concatenate([mine, theirs], axis=0),
            jnp.concatenate([theirs, mine], axis=0),
        )

    queries = ordered(own_queries, peer_queries).reshape(all_rows, local_heads, GROUP, HD)
    fresh_keys = ordered(own_keys, peer_keys)
    fresh_values = ordered(own_values, peer_values)
    state = (
        jnp.full((local_heads, GROUP, all_rows), FLOOR_SCORE, jnp.float32),
        jnp.zeros((local_heads, GROUP, all_rows), jnp.float32),
        jnp.zeros((all_rows, local_heads, GROUP, HD), jnp.float32),
    )
    token_index = jnp.arange(all_rows)
    causal = (token_index[None, :] <= token_index[:, None]) & (parity == 1)
    state = absorb(state, queries, fresh_keys, fresh_values, causal, scale)
    page_count = (length + page_rows - 1) // page_rows
    even_pages = (page_count + 1) // 2
    first_page = jnp.where(parity == 0, 0, even_pages)
    last_page = jnp.where(parity == 0, even_pages, page_count)
    table_row = jnp.concatenate([page_table[request], jnp.full((BLOCK_PAGES,), -1, jnp.int32)])
    offset = device_row * pages_local
    block_count = (last_page - first_page + BLOCK_PAGES - 1) // BLOCK_PAGES

    def visit(block, carry):
        block_first = first_page + block * BLOCK_PAGES
        logical = block_first + jnp.arange(BLOCK_PAGES)
        physical = lax.dynamic_slice(table_row, (block_first,), (BLOCK_PAGES,))
        slots = jnp.clip(physical - offset, 0, pages_local - 1)
        block_keys = k_cache[slots].reshape(block_rows, local_heads, HD)
        block_values = v_cache[slots].reshape(block_rows, local_heads, HD)
        key_places = (logical[:, None] * page_rows + jnp.arange(page_rows)[None, :]).reshape(
            block_rows
        )
        usable = jnp.repeat(logical < last_page, page_rows) & (key_places < length)
        allowed = jnp.broadcast_to(usable[None, :], (all_rows, block_rows))
        return absorb(carry, queries, block_keys, block_values, allowed, scale)

    running_max, running_sum, output = lax.fori_loop(0, block_count, visit, state)
    peer_start = (1 - parity) * own_rows
    own_start = parity * own_rows
    outgoing = (
        lax.dynamic_slice_in_dim(output, peer_start, own_rows, 0),
        lax.dynamic_slice_in_dim(running_max, peer_start, own_rows, 2),
        lax.dynamic_slice_in_dim(running_sum, peer_start, own_rows, 2),
    )
    other_output, other_max, other_sum = (
        from_partner(outgoing[0].astype(jnp.bfloat16), "req", 0).astype(jnp.float32),
        from_partner(outgoing[1].astype(jnp.bfloat16), "req", 0).astype(jnp.float32),
        from_partner(outgoing[2].astype(jnp.bfloat16), "req", 0).astype(jnp.float32),
    )
    mine_output = lax.dynamic_slice_in_dim(output, own_start, own_rows, 0)
    mine_max = lax.dynamic_slice_in_dim(running_max, own_start, own_rows, 2)
    mine_sum = lax.dynamic_slice_in_dim(running_sum, own_start, own_rows, 2)
    joint_max = jnp.maximum(mine_max, other_max)
    mine_factor = jnp.exp(mine_max - joint_max)
    other_factor = jnp.exp(other_max - joint_max)
    joint_sum = mine_sum * mine_factor + other_sum * other_factor
    joint_output = (
        mine_output * jnp.transpose(mine_factor, (2, 0, 1))[..., None]
        + other_output * jnp.transpose(other_factor, (2, 0, 1))[..., None]
    )
    attention = (
        (joint_output / jnp.transpose(joint_sum, (2, 0, 1))[..., None])
        .reshape(own_rows, local_heads * GROUP * HD)
        .astype(jnp.bfloat16)
    )
    partial_value = lax.dot_general(
        lax.all_gather(attention, "req", axis=0, tiled=True),
        w_out,
        (((1,), (1,)), ((), ())),
        preferred_element_type=jnp.float32,
    )
    return lax.all_to_all(
        tensor_total(partial_value), "req", split_axis=0, concat_axis=1, tiled=True
    )


def solution(mesh):
    in_specs = (
        P("req", "tp"),
        P("req", "tp"),
        P("req", "tp"),
        P("req", None, "tp"),
        P("req", None, "tp"),
        P(),
        P(),
        P("req", "tp"),
    )
    out_specs = P("req", None)
    return jax.shard_map(shards, mesh=mesh, in_specs=in_specs, out_specs=out_specs, check_vma=False)
```

profile of v0, /device:TPU:1, one launch (start us, length us, event | category | flops | bytes accessed | tf_op | source)
XLA Modules:
  0.0 280.3 jit_solution(12929491694747640108)
XLA Ops:
  6.5 8.9 %collective-permute-start.2 = (bf16[64,1,128]{2,0,1:T(8,128)(2,1)}, bf16[64,1,128]{2,0,1:T(8,128)(2,1)S(1)}, u32[]{:S(2)}, u32[]{:S(2)}) collective-permute-start(bf16[64,1,128]{2,0,1:T(8,128)(2,1)} %bitcast.155), channel_id=1, source_target_pairs={{0,8},{8,0},{16,24},{24,16},{32,40},{40,32},{48,56},{56,48},{64,72... | collective-permute-start | bytes 49160 | tf_op jit(solution)/shard_map/ppermute | solution.py:15
  15.5 1.3 dynamic_slice.27
  17.4 0.7 convert_bitcast_fusion
  18.4 0.8 fusion.34
  19.3 1.9 collective-permute-start
  21.2 1.0 reshape.300
  22.5 2.4 collective-permute-start.1
  25.6 0.7 fusion.57
  26.5 0.2 fusion.62
  27.0 0.2 fusion.20
  27.2 21.1 %while.14 = (s32[]{:T(128)}, f32[1,5,128]{2,1,0:T(8,128)S(1)}, f32[1,5,128]{2,1,0:T(8,128)S(1)}, f32[128,1,5,128]{0,3,2,1:T(8,128)S(1)}, s32[]{:T(128)}, /*index...) while((s32[]{:T(128)}, f32[1,5,128]{2,1,0:T(8,128)S(1)}, ...), condition=%wide.region_5.6_spmd, body=%wide.region_2.5_spmd.sunk | while | flops 170889632 | bytes 5585255 | solution.py:118
  27.4 0.7 fusion.81
  28.1 1.6 gather_fusion.1
  29.7 1.6 gather_fusion
  31.3 0.4 bitcast_reduce_fusion.2
  31.7 0.3 fusion.83
  32.0 0.5 fusion.84
  32.6 0.7 fusion.81
  33.3 1.6 gather_fusion.1
  35.0 1.6 gather_fusion
  36.6 0.4 bitcast_reduce_fusion.2
  37.0 0.3 fusion.83
  37.2 0.5 fusion.84
  37.9 0.7 fusion.81
  38.6 1.6 gather_fusion.1
  40.2 1.6 gather_fusion
  41.8 0.4 bitcast_reduce_fusion.2
  42.2 0.3 fusion.83
  42.5 0.5 fusion.84
  43.2 0.7 fusion.81
  43.9 1.6 gather_fusion.1
  45.5 1.6 gather_fusion
  47.1 0.4 bitcast_reduce_fusion.2
  47.5 0.3 fusion.83
  47.8 0.5 fusion.84
  48.5 1.9 collective-permute-start.5
  50.4 2.4 collective-permute-start.3
  52.9 1.9 collective-permute-start.4
  54.9 1.3 collective-permute-done.4
  56.4 0.8 copy.51
  57.2 85.2 %all-gather.2.cloned.1.call-done = bf16[4096,640]{1,0:T(8,128)(2,1)} async-done(((bf16[64,640]{1,0:T(8,128)(2,1)}), bf16[4096,640]{1,0:T(8,128)(2,1)}) %all-gather.2.cloned.1.call-update) | async-done | bytes 5242896 | tf_op jit(solution)/shard_map/all_gather | solution.py:148
  142.4 4.2 %convolution_convert_fusion = bf16[4096,80]{0,1:T(8,128)(2,1)S(1)} fusion(bf16[4096,640]{1,0:T(8,128)(2,1)} %all-gather.2.cloned.1.call-done, bf16[80,640]{1,0:T(8,128)(2,1)S(1)} %copy-done), kind=kOutput, calls=%fused_computation.31 | convolution fusion | flops 419758080 | bytes 6000640 | tf_op jit(solution)/shard_map/dot_general | solution.py:147
  146.6 2.5 all_to_all.14
  149.1 75.8 %all-reduce.3.cloned.1.call-done = bf16[64,64,80]{1,0,2:T(8,128)(2,1)} async-done(((bf16[64,64,80]{1,0,2:T(8,128)(2,1)}), bf16[64,64,80]{1,0,2:T(8,128)(2,1)}) %all-reduce.3.cloned.1.call-update) | async-done | bytes 655376 | tf_op jit(solution)/shard_map/psum | solution.py:51
  224.9 2.5 copy.43
  227.4 42.4 %all_to_all.19 = bf16[64,64,80]{2,1,0:T(8,128)(2,1)S(1)} all-to-all(bf16[64,64,80]{2,1,0:T(8,128)(2,1)S(1)} %copy.43), channel_id=1, replica_groups=mesh['req'=64,'tp'=8] {'req'}, dimensions={0} | all-to-all | bytes 1310720 | tf_op jit(solution)/shard_map/all_to_all | solution.py:153
  269.8 0.7 copy.44
  270.5 3.0 %all_to_all.17 = bf16[64,5120]{1,0:T(8,128)(2,1)} reshape(bf16[64,64,80]{2,1,0:T(8,128)(2,1)S(1)} %copy.44) | data formatting | bytes 1310720 | tf_op jit(solution)/shard_map/all_to_all | solution.py:153
  (60 shorter events, 2.0 us)
Async XLA Ops:
  6.5 135.9 %copy-start = (bf16[80,640]{1,0:T(8,128)(2,1)S(1)}, bf16[80,640]{1,0:T(8,128)(2,1)}, u32[]{:S(2)}) copy-start(bf16[80,640]{1,0:T(8,128)(2,1)} %param.17) | copy-start | bytes 307204
  6.5 135.9 %all-gather.2.cloned.1.call-start = ((), (), s32[]{:S(2)}) async-start(), calls=%async_computation.1 | async-start | bytes 5324800 | tf_op jit(solution)/shard_map/all_gather | solution.py:148
  6.5 20.4 %collective-permute-start.2 = (bf16[64,1,128]{2,0,1:T(8,128)(2,1)}, bf16[64,1,128]{2,0,1:T(8,128)(2,1)S(1)}, u32[]{:S(2)}, u32[]{:S(2)}) collective-permute-start(bf16[64,1,128]{2,0,1:T(8,128)(2,1)} %bitcast.155), channel_id=1, source_target_pairs={{0,8},{8,0},{16,24},{24,16},{32,40},{40,32},{48,56},{56,48},{64,72... | collective-permute-start | bytes 49160 | tf_op jit(solution)/shard_map/ppermute | solution.py:15
  19.3 7.2 %collective-permute-start = (bf16[64,1,128]{2,0,1:T(8,128)(2,1)S(1)}, bf16[64,1,128]{2,0,1:T(8,128)(2,1)S(1)}, u32[]{:S(2)}, u32[]{:S(2)}) collective-permute-start(bf16[64,1,128]{2,0,1:T(8,128)(2,1)S(1)} %bitcast.154), channel_id=1, source_target_pairs={{0,8},{8,0},{16,24},{24,16},{32,40},{40,32},{48,56},{56,48},{64,72... | collective-permute-start | bytes 49160 | tf_op jit(solution)/shard_map/ppermute | solution.py:15
  22.5 3.9 %collective-permute-start.1 = (bf16[64,5,128]{2,1,0:T(8,128)(2,1)S(1)}, bf16[64,5,128]{2,1,0:T(8,128)(2,1)S(1)}, u32[]{:S(2)}, u32[]{:S(2)}) collective-permute-start(bf16[64,5,128]{2,1,0:T(8,128)(2,1)S(1)} %fusion.25), channel_id=1, source_target_pairs={{0,8},{8,0},{16,24},{24,16},{32,40},{40,32},{48,56},{56,48},{64,72... | collective-permute-start | bytes 245768 | tf_op jit(solution)/shard_map/ppermute | solution.py:15
  25.5 1.4 copy-start.1
  48.5 6.4 %collective-permute-start.5 = (bf16[1,5,64]{2,1,0:T(8,128)(2,1)S(1)}, bf16[1,5,64]{2,1,0:T(8,128)(2,1)S(1)}, u32[]{:S(2)}, u32[]{:S(2)}) collective-permute-start(bf16[1,5,64]{2,1,0:T(8,128)(2,1)S(1)} %dynamic-slice_convert_fusion.1), channel_id=1, source_target_pairs={{0,8},{8,0},{16,24},{24,16},{32,40},{40,32},{48,56},{56,48},{64,72... | collective-permute-start | bytes 1928 | tf_op jit(solution)/shard_map/ppermute | solution.py:15
  50.4 4.5 %collective-permute-start.3 = (bf16[1,5,64]{2,1,0:T(8,128)(2,1)S(1)}, bf16[1,5,64]{2,1,0:T(8,128)(2,1)S(1)}, u32[]{:S(2)}, u32[]{:S(2)}) collective-permute-start(bf16[1,5,64]{2,1,0:T(8,128)(2,1)S(1)} %dynamic-slice_convert_fusion.2), channel_id=1, source_target_pairs={{0,8},{8,0},{16,24},{24,16},{32,40},{40,32},{48,56},{56,48},{64,72... | collective-permute-start | bytes 1928 | tf_op jit(solution)/shard_map/ppermute | solution.py:15
  52.9 3.3 %collective-permute-start.4 = (bf16[64,1,5,128]{0,3,2,1:T(8,128)(2,1)S(1)}, bf16[64,1,5,128]{0,3,2,1:T(8,128)(2,1)S(1)}, u32[]{:S(2)}, u32[]{:S(2)}) collective-permute-start(bf16[64,1,5,128]{0,3,2,1:T(8,128)(2,1)S(1)} %dynamic-slice_convert_fusion), channel_id=1, source_target_pairs={{0,8},{8,0},{16,24},{24,16},{32,40},{40,32},{48,56},{56,48},{64,72... | collective-permute-start | bytes 245768 | tf_op jit(solution)/shard_map/ppermute | solution.py:15
  57.2 167.7 %all-reduce.3.cloned.1.call-start = ((), (), s32[]{:S(2)}) async-start(), calls=%async_computation.2 | async-start | bytes 2621440 | tf_op jit(solution)/shard_map/psum | solution.py:51
Sparse Core Ops, SparseCore 0:
  57.3 85.0 all-gather.1
  149.2 75.6 all-reduce.2
where the time goes:
time: 281 us; the launch traced here: 280 us
  waiting for transfers between devices  162 us (58%)
  blocking collectives  42.4 us (15%)
  local copies, waits for them, and re-layouts  25.5 us (9%)
  starting transfers between devices  19.5 us (7%)
  between operations  15 us (5%)
  matrix products  8.07 us (3%)
  other arithmetic  7.05 us (3%)
    all_gather x1, waiting for transfers between devices, shards(): lax.all_gather(attention, 'req', axis=0, tiled=True)  85.2 us
    psum x1, waiting for transfers between devices, tensor_total(): return lax.psum(partial_value.astype(jnp.bfloat16), 'tp')  75.8 us
    all_to_all x1, blocking collectives, shards(): lax.all_to_all(tensor_total(partial_value), 'req', split_axis=0, concat_a...  42.4 us
    ppermute x6, starting transfers between devices, from_partner(): lax.ppermute(value, axis, [(i, i ^ 1 << distance) for i in range(lax.axis...  19.5 us
    gather x4, local copies, waits for them, and re-layouts, visit(): block_values = v_cache[slots].reshape(block_rows, local_heads, HD)  6.46 us
    gather x4, local copies, waits for them, and re-layouts, visit(): block_keys = k_cache[slots].reshape(block_rows, local_heads, HD)  6.46 us
    all_to_all x3, local copies, waits for them, and re-layouts, shards(): lax.all_to_all(tensor_total(partial_value), 'req', split_axis=0, concat_a...  6.1 us
  transfers between devices with their start and end apart: 8, of which 3 were waited for; matrix products, arithmetic and copies ran while one was open for 2% of the time, Pallas kernels for 0%

commit v1 on v0

--- a/solution.py
+++ b/solution.py
@@ -9,6 +9,11 @@
 BLOCK_PAGES = 4
 ROPE_BASE = 1000000.0
 FLOOR_SCORE = -1e30
+
+
+def exchange_gather(block, mesh_axis, d):
+    outgoing = jnp.stack([block] * lax.axis_size(mesh_axis))
+    return jnp.concatenate(lax.all_to_all(outgoing, mesh_axis, 0, 0), axis=d)
 
 
 def from_partner(value, axis, distance):
@@ -145,7 +150,7 @@
         .astype(jnp.bfloat16)
     )
     partial_value = lax.dot_general(
-        lax.all_gather(attention, "req", axis=0, tiled=True),
+        exchange_gather(attention, "req", 0),
         w_out,
         (((1,), (1,)), ((), ())),
         preferred_element_type=jnp.float32,

time: 281 us -> 320 us (1.14)
  blocking collectives: 42.4 us -> 168 us
  waiting for transfers between devices: 162 us -> 77.8 us
    all_to_all x0 -> x1, blocking collectives: none -> 126 us  [exchange_gather(): return jnp.concatenate(lax.all_to_all(outgoing, mesh_axis, 0, 0), axis=d)]
    all_gather x1 -> x0, waiting for transfers between devices: 85.2 us -> none  [shards(): lax.all_gather(attention, 'req', axis=0, tiled=True)]
  transfers between devices with their start and end apart: 8 -> 7, of which waited for: 3 -> 2; matrix products, arithmetic and copies ran while one was open for 2% -> 2% of each run, Pallas kernels for 0% -> 0%
where the time goes in v1:
time: 320 us; the launch traced here: 319 us
  blocking collectives  168 us (52%)
  waiting for transfers between devices  77.8 us (24%)
  local copies, waits for them, and re-layouts  25.6 us (8%)
  starting transfers between devices  19.5 us (6%)
  between operations  14.9 us (5%)
  other arithmetic  6.75 us (2%)
  matrix products  5.6 us (2%)
    all_to_all x1, blocking collectives, exchange_gather(): return jnp.concatenate(lax.all_to_all(outgoing, mesh_axis, 0, 0), axis=d)  126 us
    psum x1, waiting for transfers between devices, tensor_total(): return lax.psum(partial_value.astype(jnp.bfloat16), 'tp')  76.5 us
    all_to_all x1, blocking collectives, shards(): lax.all_to_all(tensor_total(partial_value), 'req', split_axis=0, concat_a...  42.4 us
    ppermute x6, starting transfers between devices, from_partner(): lax.ppermute(value, axis, [(i, i ^ 1 << distance) for i in range(lax.axis...  19.5 us
    gather x4, local copies, waits for them, and re-layouts, visit(): block_keys = k_cache[slots].reshape(block_rows, local_heads, HD)  6.46 us
    gather x4, local copies, waits for them, and re-layouts, visit(): block_values = v_cache[slots].reshape(block_rows, local_heads, HD)  6.46 us
  transfers between devices with their start and end apart: 7, of which 2 were waited for; matrix products, arithmetic and copies ran while one was open for 2% of the time, Pallas kernels for 0%

profile of v1, /device:TPU:1, one launch (start us, length us, event | category | flops | bytes accessed | tf_op | source)
XLA Modules:
  0.0 318.6 jit_solution(14363549617257934311)
XLA Ops:
  6.5 8.9 %collective-permute-start.2 = (bf16[64,1,128]{2,0,1:T(8,128)(2,1)}, bf16[64,1,128]{2,0,1:T(8,128)(2,1)S(1)}, u32[]{:S(2)}, u32[]{:S(2)}) collective-permute-start(bf16[64,1,128]{2,0,1:T(8,128)(2,1)} %bitcast.157), channel_id=1, source_target_pairs={{0,8},{8,0},{16,24},{24,16},{32,40},{40,32},{48,56},{56,48},{64,72... | collective-permute-start | bytes 49160 | tf_op jit(solution)/shard_map/ppermute | solution.py:20
  15.5 1.2 dynamic_slice.27
  17.3 0.7 convert_bitcast_fusion
  18.3 0.8 fusion.34
  19.1 1.9 collective-permute-start
  21.1 1.0 reshape.307
  22.4 2.4 collective-permute-start.1
  25.4 0.7 fusion.57
  26.3 0.2 fusion.62
  26.8 0.2 fusion.20
  27.0 20.8 %while.14 = (s32[]{:T(128)}, f32[1,5,128]{2,1,0:T(8,128)S(1)}, f32[1,5,128]{2,1,0:T(8,128)S(1)}, f32[128,1,5,128]{0,3,2,1:T(8,128)S(1)}, s32[]{:T(128)}, /*index...) while((s32[]{:T(128)}, f32[1,5,128]{2,1,0:T(8,128)S(1)}, ...), condition=%wide.region_5.6_spmd, body=%wide.region_2.5_spmd.sunk | while | flops 170889632 | bytes 5585255 | solution.py:123
  27.2 0.6 fusion.81
  27.8 1.6 gather_fusion.1
  29.4 1.6 gather_fusion
  31.1 0.4 bitcast_reduce_fusion.2
  31.4 0.3 fusion.83
  31.7 0.5 fusion.84
  32.4 0.6 fusion.81
  33.0 1.6 gather_fusion.1
  34.6 1.6 gather_fusion
  36.3 0.4 bitcast_reduce_fusion.2
  36.6 0.3 fusion.83
  36.9 0.5 fusion.84
  37.6 0.6 fusion.81
  38.2 1.6 gather_fusion.1
  39.8 1.6 gather_fusion
  41.5 0.4 bitcast_reduce_fusion.2
  41.8 0.3 fusion.83
  42.1 0.5 fusion.84
  42.8 0.6 fusion.81
  43.4 1.6 gather_fusion.1
  45.0 1.6 gather_fusion
  46.7 0.4 bitcast_reduce_fusion.2
  47.0 0.3 fusion.83
  47.3 0.5 fusion.84
  48.0 1.9 collective-permute-start.5
  49.9 2.4 collective-permute-start.3
  52.4 1.9 collective-permute-start.4
  54.5 1.3 collective-permute-done.4
  56.0 0.8 stack.2
  56.8 125.7 %all_to_all.24 = bf16[64,64,640]{2,1,0:T(8,128)(2,1)S(1)} all-to-all(bf16[64,64,640]{2,1,0:T(8,128)(2,1)S(1)} %stack.2), channel_id=1, replica_groups=mesh['req'=64,'tp'=8] {'req'}, dimensions={0} | all-to-all | bytes 10485760 | tf_op jit(solution)/shard_map/all_to_all | solution.py:16
  182.5 1.7 convolution_convert_fusion
  184.2 2.5 all_to_all.18
  186.7 76.5 %all-reduce.3.cloned.1.call-done = bf16[64,64,80]{1,0,2:T(8,128)(2,1)} async-done(((bf16[64,64,80]{1,0,2:T(8,128)(2,1)}), bf16[64,64,80]{1,0,2:T(8,128)(2,1)}) %all-reduce.3.cloned.1.call-update) | async-done | bytes 655376 | tf_op jit(solution)/shard_map/psum | solution.py:56
  263.2 2.5 copy.37
  265.7 42.4 %all_to_all.25 = bf16[64,64,80]{2,1,0:T(8,128)(2,1)S(1)} all-to-all(bf16[64,64,80]{2,1,0:T(8,128)(2,1)S(1)} %copy.37), channel_id=1, replica_groups=mesh['req'=64,'tp'=8] {'req'}, dimensions={0} | all-to-all | bytes 1310720 | tf_op jit(solution)/shard_map/all_to_all | solution.py:158
  308.1 0.7 copy.38
  308.7 3.0 all_to_all.21
  (59 shorter events, 2.1 us)
Async XLA Ops:
  6.5 175.9 %copy-start = (bf16[80,640]{1,0:T(8,128)(2,1)S(1)}, bf16[80,640]{1,0:T(8,128)(2,1)}, u32[]{:S(2)}) copy-start(bf16[80,640]{1,0:T(8,128)(2,1)} %param.17) | copy-start | bytes 307204
  6.5 256.6 %all-reduce.3.cloned.1.call-start = ((), (), s32[]{:S(2)}) async-start(), calls=%async_computation.2 | async-start | bytes 2621440 | tf_op jit(solution)/shard_map/psum | solution.py:56
  6.5 20.3 %collective-permute-start.2 = (bf16[64,1,128]{2,0,1:T(8,128)(2,1)}, bf16[64,1,128]{2,0,1:T(8,128)(2,1)S(1)}, u32[]{:S(2)}, u32[]{:S(2)}) collective-permute-start(bf16[64,1,128]{2,0,1:T(8,128)(2,1)} %bitcast.157), channel_id=1, source_target_pairs={{0,8},{8,0},{16,24},{24,16},{32,40},{40,32},{48,56},{56,48},{64,72... | collective-permute-start | bytes 49160 | tf_op jit(solution)/shard_map/ppermute | solution.py:20
  19.1 7.1 %collective-permute-start = (bf16[64,1,128]{2,0,1:T(8,128)(2,1)S(1)}, bf16[64,1,128]{2,0,1:T(8,128)(2,1)S(1)}, u32[]{:S(2)}, u32[]{:S(2)}) collective-permute-start(bf16[64,1,128]{2,0,1:T(8,128)(2,1)S(1)} %bitcast.156), channel_id=1, source_target_pairs={{0,8},{8,0},{16,24},{24,16},{32,40},{40,32},{48,56},{56,48},{64,72... | collective-permute-start | bytes 49160 | tf_op jit(solution)/shard_map/ppermute | solution.py:20
  22.4 3.8 %collective-permute-start.1 = (bf16[64,5,128]{2,1,0:T(8,128)(2,1)S(1)}, bf16[64,5,128]{2,1,0:T(8,128)(2,1)S(1)}, u32[]{:S(2)}, u32[]{:S(2)}) collective-permute-start(bf16[64,5,128]{2,1,0:T(8,128)(2,1)S(1)} %fusion.25), channel_id=1, source_target_pairs={{0,8},{8,0},{16,24},{24,16},{32,40},{40,32},{48,56},{56,48},{64,72... | collective-permute-start | bytes 245768 | tf_op jit(solution)/shard_map/ppermute | solution.py:20
  25.4 1.5 copy-start.1
  48.0 6.4 %collective-permute-start.5 = (bf16[1,5,64]{2,1,0:T(8,128)(2,1)S(1)}, bf16[1,5,64]{2,1,0:T(8,128)(2,1)S(1)}, u32[]{:S(2)}, u32[]{:S(2)}) collective-permute-start(bf16[1,5,64]{2,1,0:T(8,128)(2,1)S(1)} %dynamic-slice_convert_fusion.1), channel_id=1, source_target_pairs={{0,8},{8,0},{16,24},{24,16},{32,40},{40,32},{48,56},{56,48},{64,72... | collective-permute-start | bytes 1928 | tf_op jit(solution)/shard_map/ppermute | solution.py:20
  49.9 4.5 %collective-permute-start.3 = (bf16[1,5,64]{2,1,0:T(8,128)(2,1)S(1)}, bf16[1,5,64]{2,1,0:T(8,128)(2,1)S(1)}, u32[]{:S(2)}, u32[]{:S(2)}) collective-permute-start(bf16[1,5,64]{2,1,0:T(8,128)(2,1)S(1)} %dynamic-slice_convert_fusion.2), channel_id=1, source_target_pairs={{0,8},{8,0},{16,24},{24,16},{32,40},{40,32},{48,56},{56,48},{64,72... | collective-permute-start | bytes 1928 | tf_op jit(solution)/shard_map/ppermute | solution.py:20
  52.4 3.3 %collective-permute-start.4 = (bf16[64,1,5,128]{0,3,2,1:T(8,128)(2,1)S(1)}, bf16[64,1,5,128]{0,3,2,1:T(8,128)(2,1)S(1)}, u32[]{:S(2)}, u32[]{:S(2)}) collective-permute-start(bf16[64,1,5,128]{0,3,2,1:T(8,128)(2,1)S(1)} %dynamic-slice_convert_fusion), channel_id=1, source_target_pairs={{0,8},{8,0},{16,24},{24,16},{32,40},{40,32},{48,56},{56,48},{64,72... | collective-permute-start | bytes 245768 | tf_op jit(solution)/shard_map/ppermute | solution.py:20
Sparse Core Ops, SparseCore 0:
  186.8 76.3 all-reduce.2
